TPU v7x, 512 devices: a whole 4x4x16 slice. The times are simulated.
512 devices in a mesh: dp: 16 (over y, z_lo), page: 32 (over z_hi, x, core).
Axes of the slice: x: 4, y: 4, z: 16 (z_hi: 4, z_lo: 4; z = z_hi * 4 + z_lo), core: 2. Of those that a mesh axis runs over, the one named last changes fastest.
Arguments:
- queries: bfloat16 [16, 32, 128, 1024], P('dp', 'page'), may hold values from -200 to 200
- keys: bfloat16 [16, 32, 128, 1024], P('dp', 'page'), may hold values from -6 to 6
- values: bfloat16 [16, 32, 128, 1024], P('dp', 'page'), may hold values from -6 to 6
- grad_out: bfloat16 [16, 32, 128, 1024], P('dp', 'page'), may hold values from -6 to 6
- out_weight: bfloat16 [1024, 1024], P(('dp', 'page')), may hold values from -0.1875 to 0.1875
- partners: int32 [16, 2, 32], P('dp'), may hold values from 0 to 31, as said below
- block_mask: int32 [16, 32, 2, 1, 1], P('dp', 'page'), may hold values 0 or 1
- buckets: int32 [16, 32, 3, 1, 1], P('dp', 'page'), may hold values from 0 to 31
- bias_table: float32 [32, 16], replicated, may hold values from -4 to 4
Outputs:
- layer_out: bfloat16 [16, 32, 128, 1024], P('dp', 'page')
- query_grad: bfloat16 [16, 32, 128, 1024], P('dp', 'page')
- key_grad: bfloat16 [16, 32, 128, 1024], P('dp', 'page')
- value_grad: bfloat16 [16, 32, 128, 1024], P('dp', 'page')
- weight_grad: float32 [1024, 1024], P(('dp', 'page'))
Inputs may be any that keep to these rules, and one draw needn't show every extreme that they name: partners[f, r, partners[f, r, p]] = p and partners[f, r, p] != p.
All inputs are finite; a program needn't handle non-finite values. No bound on the sum of `block_mask` on one device may be relied on, other than what follows from the above.
Results may differ from a plain program's by a relative error of at most 0.025.
Values may be sent and summed in bfloat16 or wider, within the bound.
No kernel may reach another device: no remote copies, remote signals or barrier semaphores. Data moves between devices by JAX's collectives and lax.ppermute only.
A program may use at most 64 MiB of HBM per device.

v0:
```python
import math
import jax
import jax.numpy as jnp
from jax import lax
from jax.sharding import PartitionSpec as P

H = 16
BLOCK = 128
ROUNDS = 2
heads_per_step = 4
neg_large = -1e30


def head_steps(query_rows, key_set, value_set, grad_rows, bias_blocks, allowed):
    page_len, width = query_rows.shape
    key_count = key_set.shape[0]
    groups = key_count // page_len
    head_dim = width // H
    step_count = H // heads_per_step
    block_count = page_len // BLOCK
    scale = 1.0 / math.sqrt(head_dim)

    def split(array):
        return array.reshape(array.shape[0], step_count, heads_per_step, head_dim).transpose(
            1, 0, 2, 3
        )

    bias_split = bias_blocks.reshape(
        groups, block_count, block_count, step_count, heads_per_step
    ).transpose(3, 4, 1, 0, 2)
    allow_wide = allowed.transpose(1, 0, 2)[None, :, None, :, :, None]

    def one_step(inputs):
        q_part, k_part, v_part, g_part, b_part = inputs
        scores = (
            jnp.einsum("qhd,khd->hqk", q_part, k_part, preferred_element_type=jnp.float32) * scale
        )
        scores = scores.reshape(heads_per_step, block_count, BLOCK, groups, block_count, BLOCK)
        scores = scores + b_part[:, :, None, :, :, None]
        scores = jnp.where(allow_wide, scores, neg_large).reshape(
            heads_per_step, page_len, key_count
        )
        top = jnp.max(scores, axis=-1, keepdims=True)
        expo = jnp.exp(scores - top)
        prob = expo / jnp.sum(expo, axis=-1, keepdims=True)
        prob_b = prob.astype(jnp.bfloat16)
        attn_part = jnp.einsum(
            "hqk,khd->qhd", prob_b, v_part, preferred_element_type=jnp.float32
        ).astype(jnp.bfloat16)
        dprob = jnp.einsum("qhd,khd->hqk", g_part, v_part, preferred_element_type=jnp.float32)
        row_dot = jnp.sum(g_part.astype(jnp.float32) * attn_part.astype(jnp.float32), axis=-1).T[
            :, :, None
        ]
        dscore = (prob * (dprob - row_dot) * scale).astype(jnp.bfloat16)
        q_grad = jnp.einsum("hqk,khd->qhd", dscore, k_part, preferred_element_type=jnp.float32)
        k_grad = jnp.einsum("hqk,qhd->khd", dscore, q_part, preferred_element_type=jnp.float32)
        v_grad = jnp.einsum("hqk,qhd->khd", prob_b, g_part, preferred_element_type=jnp.float32)
        return (attn_part, q_grad, k_grad, v_grad)

    results = lax.map(
        one_step,
        (split(query_rows), split(key_set), split(value_set), split(grad_rows), bias_split),
    )

    def join(array):
        return array.transpose(1, 0, 2, 3).reshape(array.shape[1], width)

    return (join(results[0]), join(results[1]), join(results[2]), join(results[3]))


def shards(queries, keys, values, grad_out, out_weight, partners, block_mask, buckets, bias_table):
    weight = lax.all_gather(out_weight, ("dp", "page"), axis=0, tiled=True)
    q_page = queries[0, 0]
    k_page = keys[0, 0]
    v_page = values[0, 0]
    g_page = grad_out[0, 0]
    page_len, width = q_page.shape
    block_count = page_len // BLOCK
    peers = lax.axis_size("page")
    piece_rows = page_len // peers
    mates = partners[0]
    kv_pair = jnp.stack([k_page, v_page])
    d_attn = lax.dot_general(
        g_page, weight, (((1,), (1,)), ((), ())), preferred_element_type=jnp.float32
    ).astype(jnp.bfloat16)

    def spread(stacked):
        pieces = stacked.reshape(2, peers, piece_rows, width)
        return lax.all_to_all(pieces, "page", split_axis=1, concat_axis=1, tiled=True)

    def collect(received, chosen):
        picked = jnp.take(received, chosen, axis=1)
        back = lax.all_to_all(picked, "page", split_axis=2, concat_axis=2, tiled=True)
        return back.reshape(2, chosen.shape[0], page_len, width)

    fetched = jnp.concatenate(
        [collect(spread(kv_pair), mates[r : r + 1]) for r in range(ROUNDS)], 1
    )
    key_set = jnp.concatenate([k_page[None], fetched[0]], 0).reshape(-1, width)
    value_set = jnp.concatenate([v_page[None], fetched[1]], 0).reshape(-1, width)
    bucket_ids = buckets[0, 0]
    one_hot = bucket_ids[..., None] == jnp.arange(bias_table.shape[0], dtype=jnp.int32)
    bias_blocks = jnp.sum(jnp.where(one_hot[..., None], bias_table, 0.0), axis=-2)
    allowed = jnp.concatenate(
        [jnp.ones((1, block_count, block_count), bool), block_mask[0, 0] == 1], 0
    )
    attn, q_grad, k_grad, v_grad = head_steps(
        q_page, key_set, value_set, d_attn, bias_blocks, allowed
    )
    layer_out = jnp.dot(attn, weight, preferred_element_type=jnp.float32).astype(jnp.bfloat16)
    weight_grad = lax.psum_scatter(
        lax.dot_general(attn, g_page, (((0,), (0,)), ((), ())), preferred_element_type=jnp.float32),
        ("dp", "page"),
        scatter_dimension=0,
        tiled=True,
    )
    outgoing = (
        jnp.stack([k_grad[page_len:], v_grad[page_len:]])
        .reshape(2, ROUNDS, page_len, width)
        .astype(jnp.bfloat16)
    )

    def give_back(terms, chosen):
        round_count = terms.shape[1]
        pieces = terms.reshape(2, round_count, peers, piece_rows, width)
        received = lax.all_to_all(pieces, "page", split_axis=2, concat_axis=2, tiled=True)
        picked = jnp.stack([jnp.take(received[:, 0], chosen[0], axis=1)], 1)
        back = lax.all_to_all(picked, "page", split_axis=2, concat_axis=2, tiled=True)
        return back.reshape(2, round_count, page_len, width)

    returned = jnp.concatenate(
        [give_back(outgoing[:, r : r + 1], mates[r : r + 1]) for r in range(ROUNDS)], 1
    )
    totals = jnp.stack([k_grad[:page_len], v_grad[:page_len]]) + jnp.sum(
        returned.astype(jnp.float32), axis=1
    )
    key_grad = totals[0].astype(jnp.bfloat16)[None, None]
    value_grad = totals[1].astype(jnp.bfloat16)[None, None]
    return (
        layer_out[None, None],
        q_grad.astype(jnp.bfloat16)[None, None],
        key_grad,
        value_grad,
        weight_grad,
    )


def solution(mesh):
    in_specs = (
        P("dp", "page", None, None),
        P("dp", "page", None, None),
        P("dp", "page", None, None),
        P("dp", "page", None, None),
        P(("dp", "page"), None),
        P("dp", None, None),
        P("dp", "page", None, None, None),
        P("dp", "page", None, None, None),
        P(),
    )
    out_specs = (
        P("dp", "page", None, None),
        P("dp", "page", None, None),
        P("dp", "page", None, None),
        P("dp", "page", None, None),
        P(("dp", "page"), None),
    )
    return jax.shard_map(shards, mesh=mesh, in_specs=in_specs, out_specs=out_specs, check_vma=False)
```

profile of v0, /device:TPU:2, one launch (start us, length us, event | category | flops | bytes accessed | tf_op | source)
XLA Modules:
  0.0 1547.2 jit_solution(18248375689373877247)
XLA Ops:
  7.2 1.1 stack.31
  9.4 1.1 pad_maximum_fusion.4
  10.5 18.2 %all-to-all-start = ((bf16[2,32,4,1024]{3,2,0,1:T(4,128)(2,1)}), bf16[2,32,4,1024]{3,2,0,1:T(4,128)(2,1)S(1)}, u32[]{:S(2)}, u32[]{:S(2)}) async-start(bf16[2,32,4,1024]{3,2,0,1:T(4,128)(2,1)} %pad_maximum_fusion.4), calls=%async_computation | async-start | bytes 1048576 | tf_op jit(solution)/shard_map/all_to_all | solution.py:89
  28.8 27.8 %all-to-all-done = bf16[2,32,4,1024]{3,2,0,1:T(4,128)(2,1)S(1)} async-done(((bf16[2,32,4,1024]{3,2,0,1:T(4,128)(2,1)}), bf16[2,32,4,1024]{3,2,0,1:T(4,128)(2,1)S(1)}, u32[]{:S(2)}, u32[]{:S(2)}) %all-to-all-start) | async-done | bytes 524320 | tf_op jit(solution)/shard_map/all_to_all | solution.py:89
  57.8 1.1 fusion.71
  58.9 10.8 all-to-all-start.1
  71.6 1.1 fusion.70
  72.7 25.7 %all-to-all-done.1 = bf16[2,1,32,4,1024]{4,3,0,1,2:T(4,128)(2,1)S(1)} async-done(((bf16[2,1,32,4,1024]{4,3,0,1,2:T(4,128)(2,1)}), bf16[2,1,32,4,1024]{4,3,0,1,2:T(4,128)(2,1)S(1)}, u32[]{:S(2)}, u32[]{:S(2)}) %all-to-all-start.1) | async-done | bytes 524320 | tf_op jit(solution)/shard_map/all_to_all | solution.py:93
  98.4 10.6 all-to-all-start.2
  111.2 25.7 %all-to-all-done.2 = bf16[2,1,32,4,1024]{4,3,0,1,2:T(4,128)(2,1)S(1)} async-done(((bf16[2,1,32,4,1024]{4,3,0,1,2:T(4,128)(2,1)}), bf16[2,1,32,4,1024]{4,3,0,1,2:T(4,128)(2,1)S(1)}, u32[]{:S(2)}, u32[]{:S(2)}) %all-to-all-start.2) | async-done | bytes 524320 | tf_op jit(solution)/shard_map/all_to_all | solution.py:93
  137.4 1.8 pad_maximum_fusion
  141.0 1.5 reshape_reshape.6
  144.2 712.5 %all-gather.3.cloned.1.call-done = bf16[512,2,1024]{2,1,0:T(2,128)(2,1)} async-done(((bf16[1,2,1024]{2,1,0:T(2,128)(2,1)}), bf16[512,2,1024]{2,1,0:T(2,128)(2,1)}) %all-gather.3.cloned.1.call-update) | async-done | bytes 2097168 | tf_op jit(solution)/shard_map/all_gather | solution.py:72
  856.7 2.7 reshape.233
  861.2 50.1 %while.16 = (s32[]{:T(128)}, bf16[4,128,4,64]{1,3,2,0:T(8,128)(2,1)}, bf16[4,128,4,64]{1,3,2,0:T(8,128)(2,1)}, f32[4,384,4,64]{1,3,2,0:T(8,128)}, f32[4,384,4,64...) while((s32[]{:T(128)}, ...), condition=%wide.region_5.7_spmd, body=%wide.region_1.6_spmd.sunk | while | flops 205817472 | bytes 5562152 | solution.py:60
  861.9 2.1 fusion.126
  864.1 2.2 bitcast_dynamic-update-slice_fusion.2
  867.1 1.6 fusion.127
  868.7 1.8 fusion.129
  870.6 2.2 fusion.130
  874.5 2.1 fusion.126
  876.6 2.2 bitcast_dynamic-update-slice_fusion.2
  879.7 1.6 fusion.127
  881.3 1.8 fusion.129
  883.1 2.3 fusion.130
  887.0 2.1 fusion.126
  889.2 2.2 bitcast_dynamic-update-slice_fusion.2
  892.2 1.6 fusion.127
  893.8 1.8 fusion.129
  895.6 2.2 fusion.130
  899.5 2.1 fusion.126
  901.7 2.2 bitcast_dynamic-update-slice_fusion.2
  904.7 1.6 fusion.127
  906.3 1.8 fusion.129
  908.2 2.2 fusion.130
  911.3 1.3 slice.107
  913.5 2.7 copy.125
  916.2 2.1 slice.106
  918.3 2.0 stack.38
  920.3 3.8 copy.126
  924.1 3.9 fusion.69
  929.1 8.3 all-to-all-start.3
  938.5 27.1 %all-to-all-done.3 = bf16[2,1,32,4,1024]{4,3,0,1,2:T(4,128)(2,1)S(1)} async-done(((bf16[2,1,32,4,1024]{4,3,0,1,2:T(4,128)(2,1)}), bf16[2,1,32,4,1024]{4,3,0,1,2:T(4,128)(2,1)S(1)}, u32[]{:S(2)}, u32[]{:S(2)}) %all-to-all-start.3) | async-done | bytes 524320 | tf_op jit(solution)/shard_map/all_to_all | solution.py:126
  965.6 10.5 all-to-all-start.5
  977.2 2.0 gather_fusion.2
  979.2 1.1 select_bitcast_fusion.1
  980.3 24.5 %all-to-all-done.5 = bf16[2,1,32,4,1024]{4,3,0,1,2:T(4,128)(2,1)S(1)} async-done(((bf16[2,1,32,4,1024]{4,3,0,1,2:T(4,128)(2,1)}), bf16[2,1,32,4,1024]{4,3,0,1,2:T(4,128)(2,1)S(1)}, u32[]{:S(2)}, u32[]{:S(2)}) %all-to-all-start.5) | async-done | bytes 524320 | tf_op jit(solution)/shard_map/all_to_all | solution.py:126
  1004.8 10.4 all-to-all-start.4
  1015.5 3.6 fusion.72
  1020.1 2.0 gather_fusion.3
  1022.1 1.1 select_bitcast_fusion
  1023.2 20.7 %all-to-all-done.4 = bf16[2,1,32,4,1024]{4,3,0,1,2:T(4,128)(2,1)S(1)} async-done(((bf16[2,1,32,4,1024]{4,3,0,1,2:T(4,128)(2,1)}), bf16[2,1,32,4,1024]{4,3,0,1,2:T(4,128)(2,1)S(1)}, u32[]{:S(2)}, u32[]{:S(2)}) %all-to-all-start.4) | async-done | bytes 524320 | tf_op jit(solution)/shard_map/all_to_all | solution.py:128
  1044.0 10.6 all-to-all-start.6
  1054.6 1.1 slice.76
  1055.7 1.9 slice.77
  1058.1 1.3 copy.124
  1059.4 1.8 copy.135
  1061.2 2.1 fusion.67
  1063.3 467.6 %all-reduce.3.cloned.1.call-done = f32[1024,1024]{1,0:T(8,128)} async-done(((f32[1024,1024]{1,0:T(8,128)}), f32[1024,1024]{1,0:T(8,128)}) %all-reduce.3.cloned.1.call-update) | async-done | bytes 4194320
  1530.9 1.4 constant_dynamic-slice_fusion.1
  1532.3 1.5 copy.130
  1533.8 1.6 copy.134
  1535.4 1.5 convert_reduce_fusion
  1536.9 1.1 fusion.68
  (107 shorter events, 30.0 us)
Async XLA Ops:
  7.2 852.3 %copy-start = (bf16[1,1,128,1024]{3,2,1,0:T(8,128)(2,1)S(1)}, bf16[1,1,128,1024]{3,2,1,0:T(8,128)(2,1)}, u32[]{:S(2)}) copy-start(bf16[1,1,128,1024]{3,2,1,0:T(8,128)(2,1)} %param.18) | copy-start | bytes 786436
  7.2 21.6 %copy-start.6 = (s32[1,2,32]{2,1,0:T(2,128)S(1)}, s32[1,2,32]{2,1,0:T(2,128)}, u32[]{:S(2)}) copy-start(s32[1,2,32]{2,1,0:T(2,128)} %param.20) | copy-start | bytes 772
  10.5 46.2 %all-to-all-start = ((bf16[2,32,4,1024]{3,2,0,1:T(4,128)(2,1)}), bf16[2,32,4,1024]{3,2,0,1:T(4,128)(2,1)S(1)}, u32[]{:S(2)}, u32[]{:S(2)}) async-start(bf16[2,32,4,1024]{3,2,0,1:T(4,128)(2,1)} %pad_maximum_fusion.4), calls=%async_computation | async-start | bytes 1048576 | tf_op jit(solution)/shard_map/all_to_all | solution.py:89
  58.9 39.4 %all-to-all-start.1 = ((bf16[2,1,32,4,1024]{4,3,0,1,2:T(4,128)(2,1)}), bf16[2,1,32,4,1024]{4,3,0,1,2:T(4,128)(2,1)S(1)}, u32[]{:S(2)}, u32[]{:S(2)}) async-start(bf16[2,1,32,4,1024]{4,3,0,1,2:T(4,128)(2,1)} %fusion.71), calls=%async_computation.1 | async-start | bytes 1048576 | tf_op jit(solution)/shard_map/all_to_all | solution.py:93
  69.8 786.9 %all-gather.3.cloned.1.call-start = ((), (), s32[]{:S(2)}) async-start(), calls=%async_computation.7 | async-start | bytes 2101248 | tf_op jit(solution)/shard_map/all_gather | solution.py:72
  70.5 38.5 %copy-start.5 = (bf16[1,1,128,1024]{3,2,1,0:T(8,128)(2,1)S(1)}, bf16[1,1,128,1024]{3,2,1,0:T(8,128)(2,1)}, u32[]{:S(2)}) copy-start(bf16[1,1,128,1024]{3,2,1,0:T(8,128)(2,1)} %param.15) | copy-start | bytes 786436
  71.5 38.3 %copy-start.9 = (s32[1,1,3,1,1]{2,4,3,1,0:T(1,128)S(1)}, s32[1,1,3,1,1]{2,4,3,1,0:T(1,128)}, u32[]{:S(2)}) copy-start(s32[1,1,3,1,1]{2,4,3,1,0:T(1,128)} %param.22) | copy-start | bytes 40
  71.6 38.4 %copy-start.8 = (f32[32,16]{0,1:T(8,128)S(1)}, f32[32,16]{0,1:T(8,128)}, u32[]{:S(2)}) copy-start(f32[32,16]{0,1:T(8,128)} %param.23) | copy-start | bytes 6148
  71.6 38.5 %copy-start.10 = (s32[1,1,2,1,1]{2,4,3,1,0:T(1,128)S(1)}, s32[1,1,2,1,1]{2,4,3,1,0:T(1,128)}, u32[]{:S(2)}) copy-start(s32[1,1,2,1,1]{2,4,3,1,0:T(1,128)} %param.21) | copy-start | bytes 28
  98.4 38.5 %all-to-all-start.2 = ((bf16[2,1,32,4,1024]{4,3,0,1,2:T(4,128)(2,1)}), bf16[2,1,32,4,1024]{4,3,0,1,2:T(4,128)(2,1)S(1)}, u32[]{:S(2)}, u32[]{:S(2)}) async-start(bf16[2,1,32,4,1024]{4,3,0,1,2:T(4,128)(2,1)} %fusion.70), calls=%async_computation.2 | async-start | bytes 1048576 | tf_op jit(solution)/shard_map/all_to_all | solution.py:93
  139.2 1.0 copy-start.3
  141.0 1.7 copy-start.4
  861.9 4.3 copy-start.11
  864.1 2.2 copy-start.12
  874.5 4.3 copy-start.11
  876.6 2.2 copy-start.12
  887.0 4.3 copy-start.11
  889.2 2.2 copy-start.12
  899.5 4.3 copy-start.11
  901.7 2.2 copy-start.12
  928.0 9.4 copy-start.2
  929.1 47.0 %copy-start.7 = (s32[1,2,32]{2,1,0:T(2,128)S(1)}, s32[1,2,32]{2,1,0:T(2,128)}, u32[]{:S(2)}) copy-start(s32[1,2,32]{2,1,0:T(2,128)} %param.20) | copy-start | bytes 772
  929.1 36.5 %all-to-all-start.3 = ((bf16[2,1,32,4,1024]{4,3,0,1,2:T(4,128)(2,1)}), bf16[2,1,32,4,1024]{4,3,0,1,2:T(4,128)(2,1)S(1)}, u32[]{:S(2)}, u32[]{:S(2)}) async-start(bf16[2,1,32,4,1024]{4,3,0,1,2:T(4,128)(2,1)} %copy.127), calls=%async_computation.3 | async-start | bytes 1048576 | tf_op jit(solution)/shard_map/all_to_all | solution.py:126
  965.6 39.2 %all-to-all-start.5 = ((bf16[2,1,32,4,1024]{4,3,0,1,2:T(4,128)(2,1)}), bf16[2,1,32,4,1024]{4,3,0,1,2:T(4,128)(2,1)S(1)}, u32[]{:S(2)}, u32[]{:S(2)}) async-start(bf16[2,1,32,4,1024]{4,3,0,1,2:T(4,128)(2,1)} %copy.131), calls=%async_computation.5 | async-start | bytes 1048576 | tf_op jit(solution)/shard_map/all_to_all | solution.py:126
  1004.8 39.2 %all-to-all-start.4 = ((bf16[2,1,32,4,1024]{4,3,0,1,2:T(4,128)(2,1)}), bf16[2,1,32,4,1024]{4,3,0,1,2:T(4,128)(2,1)S(1)}, u32[]{:S(2)}, u32[]{:S(2)}) async-start(bf16[2,1,32,4,1024]{4,3,0,1,2:T(4,128)(2,1)} %select_bitcast_fusion.1), calls=%async_computation.4 | async-start | bytes 1048576 | tf_op jit(solution)/shard_map/all_to_all | solution.py:128
  1015.2 515.7 %all-reduce.3.cloned.1.call-start = ((), (), s32[]{:S(2)}) async-start(), calls=%async_computation.8 | async-start | bytes 8388608
  1044.0 13.7 copy-start.1
  1044.0 489.9 %all-to-all-start.6 = ((bf16[2,1,32,4,1024]{4,3,0,1,2:T(4,128)(2,1)}), bf16[2,1,32,4,1024]{4,3,0,1,2:T(4,128)(2,1)}, u32[]{:S(2)}, u32[]{:S(2)}) async-start(bf16[2,1,32,4,1024]{4,3,0,1,2:T(4,128)(2,1)} %select_bitcast_fusion), calls=%async_computation.6 | async-start | bytes 1048576 | tf_op jit(solution)/shard_map/all_to_all | solution.py:128
Sparse Core Ops, SparseCore 0:
  72.7 783.9 all-gather.2
  1021.4 509.4 all-reduce.2
where the time goes:
time: 1550 us
  waiting for transfers between devices  1330 us (86%)
  starting transfers between devices  79.8 us (5%)
  local copies, waits for them, and re-layouts  51.8 us (3%)
  matrix products  50.2 us (3%)
  other arithmetic  18.3 us (1%)
    all_gather x1, waiting for transfers between devices, shards(): weight = lax.all_gather(out_weight, ('dp', 'page'), axis=0, tiled=True)  713 us
    unnamed x3, waiting for transfers between devices  468 us
    all_to_all x2, waiting for transfers between devices, give_back(): lax.all_to_all(pieces, 'page', split_axis=2, concat_axis=2, tiled=True)  51.6 us
    all_to_all x2, waiting for transfers between devices, collect(): lax.all_to_all(picked, 'page', split_axis=2, concat_axis=2, tiled=True)  51.4 us
  transfers between devices with their start and end apart: 9, of which 8 were waited for; matrix products, arithmetic and copies ran while one was open for 2% of the time, Pallas kernels for 0%

commit v1 on v0

--- a/solution.py
+++ b/solution.py
@@ -123,7 +123,12 @@
     def give_back(terms, chosen):
         round_count = terms.shape[1]
         pieces = terms.reshape(2, round_count, peers, piece_rows, width)
-        received = lax.all_to_all(pieces, "page", split_axis=2, concat_axis=2, tiled=True)
+        received = jnp.concatenate(
+            lax.all_to_all(
+                jnp.stack(jnp.split(pieces, lax.axis_size("page"), axis=2)), "page", 0, 0
+            ),
+            axis=2,
+        )
         picked = jnp.stack([jnp.take(received[:, 0], chosen[0], axis=1)], 1)
         back = lax.all_to_all(picked, "page", split_axis=2, concat_axis=2, tiled=True)
         return back.reshape(2, round_count, page_len, width)

time: 1550 us -> 1570 us (1.013)
  local copies, waits for them, and re-layouts: 51.8 us -> 84.5 us
  waiting for transfers between devices: 1330 us -> 1310 us
    unnamed x30 -> x92, local copies, waits for them, and re-layouts: 9.48 us -> 47.4 us
    all_to_all x2, waiting for transfers between devices: 51.6 us -> 32.7 us  [give_back(): lax.all_to_all(jnp.stack(jnp.split(pieces, lax.axis_size('page'), axis=2)...]
  transfers between devices with their start and end apart: 9 -> 9, of which waited for: 8 -> 8; matrix products, arithmetic and copies ran while one was open for 2% -> 3% of each run, Pallas kernels for 0% -> 0%
where the time goes in v1:
time: 1570 us; the launch traced here: 1560 us
  waiting for transfers between devices  1310 us (83%)
  local copies, waits for them, and re-layouts  84.5 us (5%)
  starting transfers between devices  79.6 us (5%)
  matrix products  50.2 us (3%)
  other arithmetic  22.7 us (1%)
    all_gather x1, waiting for transfers between devices, shards(): weight = lax.all_gather(out_weight, ('dp', 'page'), axis=0, tiled=True)  713 us
    unnamed x3, waiting for transfers between devices  469 us
    all_to_all x2, waiting for transfers between devices, collect(): lax.all_to_all(picked, 'page', split_axis=2, concat_axis=2, tiled=True)  51.4 us
    unnamed x92, local copies, waits for them, and re-layouts  47.4 us
    all_to_all x2, waiting for transfers between devices, give_back(): lax.all_to_all(jnp.stack(jnp.split(pieces, lax.axis_size('page'), axis=2)...  32.7 us
  transfers between devices with their start and end apart: 9, of which 8 were waited for; matrix products, arithmetic and copies ran while one was open for 3% of the time, Pallas kernels for 0%

profile of v1, /device:TPU:2, one launch (start us, length us, event | category | flops | bytes accessed | tf_op | source)
XLA Modules:
  0.0 1564.4 jit_solution(8226999290201410836)
XLA Ops:
  7.2 1.1 stack.229
  8.3 1.1 stack.230
  9.4 1.1 pad_maximum_fusion.4
  10.5 18.2 %all-to-all-start = ((bf16[2,32,4,1024]{3,2,0,1:T(4,128)(2,1)}), bf16[2,32,4,1024]{3,2,0,1:T(4,128)(2,1)S(1)}, u32[]{:S(2)}, u32[]{:S(2)}) async-start(bf16[2,32,4,1024]{3,2,0,1:T(4,128)(2,1)} %pad_maximum_fusion.4), calls=%async_computation | async-start | bytes 1048576 | tf_op jit(solution)/shard_map/all_to_all | solution.py:89
  28.8 27.8 %all-to-all-done = bf16[2,32,4,1024]{3,2,0,1:T(4,128)(2,1)S(1)} async-done(((bf16[2,32,4,1024]{3,2,0,1:T(4,128)(2,1)}), bf16[2,32,4,1024]{3,2,0,1:T(4,128)(2,1)S(1)}, u32[]{:S(2)}, u32[]{:S(2)}) %all-to-all-start) | async-done | bytes 524320 | tf_op jit(solution)/shard_map/all_to_all | solution.py:89
  56.8 1.0 gather_fusion
  57.8 1.1 fusion.71
  58.9 10.8 all-to-all-start.1
  71.6 1.1 fusion.70
  72.7 25.7 %all-to-all-done.1 = bf16[2,1,32,4,1024]{4,3,0,1,2:T(4,128)(2,1)S(1)} async-done(((bf16[2,1,32,4,1024]{4,3,0,1,2:T(4,128)(2,1)}), bf16[2,1,32,4,1024]{4,3,0,1,2:T(4,128)(2,1)S(1)}, u32[]{:S(2)}, u32[]{:S(2)}) %all-to-all-start.1) | async-done | bytes 524320 | tf_op jit(solution)/shard_map/all_to_all | solution.py:93
  98.4 10.6 all-to-all-start.2
  111.2 25.7 %all-to-all-done.2 = bf16[2,1,32,4,1024]{4,3,0,1,2:T(4,128)(2,1)S(1)} async-done(((bf16[2,1,32,4,1024]{4,3,0,1,2:T(4,128)(2,1)}), bf16[2,1,32,4,1024]{4,3,0,1,2:T(4,128)(2,1)S(1)}, u32[]{:S(2)}, u32[]{:S(2)}) %all-to-all-start.2) | async-done | bytes 524320 | tf_op jit(solution)/shard_map/all_to_all | solution.py:93
  137.4 1.8 pad_maximum_fusion
  141.0 1.5 reshape_reshape.6
  144.2 712.5 %all-gather.3.cloned.1.call-done = bf16[512,2,1024]{2,1,0:T(2,128)(2,1)} async-done(((bf16[1,2,1024]{2,1,0:T(2,128)(2,1)}), bf16[512,2,1024]{2,1,0:T(2,128)(2,1)}) %all-gather.3.cloned.1.call-update) | async-done | bytes 2097168 | tf_op jit(solution)/shard_map/all_gather | solution.py:72
  856.7 2.7 reshape.241
  861.2 50.1 %while.16 = (s32[]{:T(128)}, bf16[4,128,4,64]{1,3,2,0:T(8,128)(2,1)}, bf16[4,128,4,64]{1,3,2,0:T(8,128)(2,1)}, f32[4,384,4,64]{1,3,2,0:T(8,128)}, f32[4,384,4,64...) while((s32[]{:T(128)}, ...), condition=%wide.region_5.7_spmd, body=%wide.region_1.6_spmd.sunk | while | flops 205817472 | bytes 5562152 | solution.py:60
  861.9 2.1 fusion.128
  864.1 2.2 bitcast_dynamic-update-slice_fusion.2
  867.1 1.6 fusion.129
  868.7 1.8 fusion.131
  870.6 2.2 fusion.132
  874.5 2.1 fusion.128
  876.6 2.2 bitcast_dynamic-update-slice_fusion.2
  879.7 1.6 fusion.129
  881.3 1.8 fusion.131
  883.1 2.3 fusion.132
  887.0 2.1 fusion.128
  889.2 2.2 bitcast_dynamic-update-slice_fusion.2
  892.2 1.6 fusion.129
  893.8 1.8 fusion.131
  895.6 2.2 fusion.132
  899.5 2.1 fusion.128
  901.7 2.2 bitcast_dynamic-update-slice_fusion.2
  904.7 1.6 fusion.129
  906.3 1.8 fusion.131
  908.2 2.2 fusion.132
  911.3 1.3 slice.107
  913.5 2.7 copy.183
  916.2 2.1 slice.106
  918.3 2.0 stack.236
  920.3 3.8 copy.184
  924.1 3.9 fusion.69
  947.6 8.3 all-to-all-start.3
  975.5 8.7 all-to-all-done.3
  984.2 10.5 all-to-all-start.5
  994.7 2.4 gather_fusion.2
  997.1 2.4 fusion.72
  999.5 23.9 %all-to-all-done.5 = bf16[32,2,1,1,4,1024]{5,1,4,3,2,0:T(2,128)(2,1)S(1)} async-done(((bf16[32,2,1,1,4,1024]{5,1,4,3,2,0:T(2,128)(2,1)}), bf16[32,2,1,1,4,1024]{5,1,4,3,2,0:T(2,128)(2,1)S(1)}, u32[]{:S(2)}, u32[]{:S(2)}) %all-to-all-start.5) | async-done | bytes 524320 | tf_op jit(solution)/shard_map/all_to_all | solution.py:127
  1023.4 10.3 all-to-all-start.4
  1033.8 3.6 fusion.74
  1037.4 2.4 gather_fusion.3
  1039.8 2.5 fusion.73
  1042.3 19.7 %all-to-all-done.4 = bf16[2,1,32,4,1024]{4,0,3,1,2:T(2,128)(2,1)S(1)} async-done(((bf16[2,1,32,4,1024]{4,0,3,1,2:T(2,128)(2,1)}), bf16[2,1,32,4,1024]{4,0,3,1,2:T(2,128)(2,1)S(1)}, u32[]{:S(2)}, u32[]{:S(2)}) %all-to-all-start.4) | async-done | bytes 524320 | tf_op jit(solution)/shard_map/all_to_all | solution.py:133
  1062.0 10.9 all-to-all-start.6
  1072.9 1.1 slice.76
  1074.0 1.9 slice.77
  1076.4 1.3 copy.182
  1077.7 1.8 copy.191
  1079.5 2.1 fusion.67
  1081.6 468.0 %all-reduce.3.cloned.1.call-done = f32[1024,1024]{1,0:T(8,128)} async-done(((f32[1024,1024]{1,0:T(8,128)}), f32[1024,1024]{1,0:T(8,128)}) %all-reduce.3.cloned.1.call-update) | async-done | bytes 4194320
  1549.6 1.4 constant_dynamic-slice_fusion.1
  1551.0 3.2 convert_reduce_fusion
  1554.1 1.1 fusion.68
  (165 shorter events, 62.7 us)
Async XLA Ops:
  7.2 852.3 %copy-start = (bf16[1,1,128,1024]{3,2,1,0:T(8,128)(2,1)S(1)}, bf16[1,1,128,1024]{3,2,1,0:T(8,128)(2,1)}, u32[]{:S(2)}) copy-start(bf16[1,1,128,1024]{3,2,1,0:T(8,128)(2,1)} %param.18) | copy-start | bytes 786436
  7.2 21.6 %copy-start.6 = (s32[1,2,32]{2,1,0:T(2,128)S(1)}, s32[1,2,32]{2,1,0:T(2,128)}, u32[]{:S(2)}) copy-start(s32[1,2,32]{2,1,0:T(2,128)} %param.20) | copy-start | bytes 772
  10.5 46.2 %all-to-all-start = ((bf16[2,32,4,1024]{3,2,0,1:T(4,128)(2,1)}), bf16[2,32,4,1024]{3,2,0,1:T(4,128)(2,1)S(1)}, u32[]{:S(2)}, u32[]{:S(2)}) async-start(bf16[2,32,4,1024]{3,2,0,1:T(4,128)(2,1)} %pad_maximum_fusion.4), calls=%async_computation | async-start | bytes 1048576 | tf_op jit(solution)/shard_map/all_to_all | solution.py:89
  58.9 39.4 %all-to-all-start.1 = ((bf16[2,1,32,4,1024]{4,3,0,1,2:T(4,128)(2,1)}), bf16[2,1,32,4,1024]{4,3,0,1,2:T(4,128)(2,1)S(1)}, u32[]{:S(2)}, u32[]{:S(2)}) async-start(bf16[2,1,32,4,1024]{4,3,0,1,2:T(4,128)(2,1)} %fusion.71), calls=%async_computation.1 | async-start | bytes 1048576 | tf_op jit(solution)/shard_map/all_to_all | solution.py:93
  69.8 786.9 %all-gather.3.cloned.1.call-start = ((), (), s32[]{:S(2)}) async-start(), calls=%async_computation.7 | async-start | bytes 2101248 | tf_op jit(solution)/shard_map/all_gather | solution.py:72
  70.5 38.5 %copy-start.5 = (bf16[1,1,128,1024]{3,2,1,0:T(8,128)(2,1)S(1)}, bf16[1,1,128,1024]{3,2,1,0:T(8,128)(2,1)}, u32[]{:S(2)}) copy-start(bf16[1,1,128,1024]{3,2,1,0:T(8,128)(2,1)} %param.15) | copy-start | bytes 786436
  71.5 38.3 %copy-start.9 = (s32[1,1,3,1,1]{2,4,3,1,0:T(1,128)S(1)}, s32[1,1,3,1,1]{2,4,3,1,0:T(1,128)}, u32[]{:S(2)}) copy-start(s32[1,1,3,1,1]{2,4,3,1,0:T(1,128)} %param.22) | copy-start | bytes 40
  71.6 38.4 %copy-start.8 = (f32[32,16]{0,1:T(8,128)S(1)}, f32[32,16]{0,1:T(8,128)}, u32[]{:S(2)}) copy-start(f32[32,16]{0,1:T(8,128)} %param.23) | copy-start | bytes 6148
  71.6 38.5 %copy-start.10 = (s32[1,1,2,1,1]{2,4,3,1,0:T(1,128)S(1)}, s32[1,1,2,1,1]{2,4,3,1,0:T(1,128)}, u32[]{:S(2)}) copy-start(s32[1,1,2,1,1]{2,4,3,1,0:T(1,128)} %param.21) | copy-start | bytes 28
  98.4 38.5 %all-to-all-start.2 = ((bf16[2,1,32,4,1024]{4,3,0,1,2:T(4,128)(2,1)}), bf16[2,1,32,4,1024]{4,3,0,1,2:T(4,128)(2,1)S(1)}, u32[]{:S(2)}, u32[]{:S(2)}) async-start(bf16[2,1,32,4,1024]{4,3,0,1,2:T(4,128)(2,1)} %fusion.70), calls=%async_computation.2 | async-start | bytes 1048576 | tf_op jit(solution)/shard_map/all_to_all | solution.py:93
  139.2 1.0 copy-start.3
  141.0 1.7 copy-start.4
  861.9 4.3 copy-start.11
  864.1 2.2 copy-start.12
  874.5 4.3 copy-start.11
  876.6 2.2 copy-start.12
  887.0 4.3 copy-start.11
  889.2 2.2 copy-start.12
  899.5 4.3 copy-start.11
  901.7 2.2 copy-start.12
  928.0 27.9 %copy-start.1 = (bf16[2,1,128,1024]{3,0,2,1:T(2,128)(2,1)S(1)}, bf16[2,1,128,1024]{3,0,2,1:T(2,128)(2,1)}, u32[]{:S(2)}) copy-start(bf16[2,1,128,1024]{3,0,2,1:T(2,128)(2,1)} %get-tuple-element.193) | copy-start | bytes 1572868
  947.6 47.0 %copy-start.7 = (s32[1,2,32]{2,1,0:T(2,128)S(1)}, s32[1,2,32]{2,1,0:T(2,128)}, u32[]{:S(2)}) copy-start(s32[1,2,32]{2,1,0:T(2,128)} %param.20) | copy-start | bytes 772
  947.6 36.6 %all-to-all-start.3 = ((bf16[32,2,1,1,4,1024]{5,1,4,3,2,0:T(2,128)(2,1)}), bf16[32,2,1,1,4,1024]{5,1,4,3,2,0:T(2,128)(2,1)S(1)}, u32[]{:S(2)}, u32[]{:S(2)}) async-start(bf16[32,2,1,1,4,1024]{5,1,4,3,2,0:T(2,128)(2,1)} %constant_dynamic-update-slice_fusion), calls=%async_computation.3 | async-start | bytes 1048576 | tf_op jit(solution)/shard_map/all_to_all | solution.py:127
  984.2 39.2 %all-to-all-start.5 = ((bf16[32,2,1,1,4,1024]{5,1,4,3,2,0:T(2,128)(2,1)}), bf16[32,2,1,1,4,1024]{5,1,4,3,2,0:T(2,128)(2,1)S(1)}, u32[]{:S(2)}, u32[]{:S(2)}) async-start(bf16[32,2,1,1,4,1024]{5,1,4,3,2,0:T(2,128)(2,1)} %constant_dynamic-update-slice_fusion.32), calls=%async_computation.5 | async-start | bytes 1048576 | tf_op jit(solution)/shard_map/all_to_all | solution.py:127
  1023.4 38.6 %all-to-all-start.4 = ((bf16[2,1,32,4,1024]{4,0,3,1,2:T(2,128)(2,1)}), bf16[2,1,32,4,1024]{4,0,3,1,2:T(2,128)(2,1)S(1)}, u32[]{:S(2)}, u32[]{:S(2)}) async-start(bf16[2,1,32,4,1024]{4,0,3,1,2:T(2,128)(2,1)} %fusion.72), calls=%async_computation.4 | async-start | bytes 1048576 | tf_op jit(solution)/shard_map/all_to_all | solution.py:133
  1033.7 515.9 %all-reduce.3.cloned.1.call-start = ((), (), s32[]{:S(2)}) async-start(), calls=%async_computation.8 | async-start | bytes 8388608
  1062.0 10.9 copy-start.2
  1062.0 488.9 %all-to-all-start.6 = ((bf16[2,1,32,4,1024]{4,0,3,1,2:T(2,128)(2,1)}), bf16[2,1,32,4,1024]{4,0,3,1,2:T(2,128)(2,1)}, u32[]{:S(2)}, u32[]{:S(2)}) async-start(bf16[2,1,32,4,1024]{4,0,3,1,2:T(2,128)(2,1)} %fusion.73), calls=%async_computation.6 | async-start | bytes 1048576 | tf_op jit(solution)/shard_map/all_to_all | solution.py:133
Sparse Core Ops, SparseCore 0:
  72.7 783.9 all-gather.2
  1040.0 509.5 all-reduce.2
